TPU v7x, 256 devices: a whole 4x4x8 slice. The times are simulated.
256 devices in a mesh: segment: 2 (over y_hi), blk: 32 (over z, x), mp: 4 (over y_lo, core).
Axes of the slice: x: 4, y: 4 (y_hi: 2, y_lo: 2; y = y_hi * 2 + y_lo), z: 8, core: 2. Of those that a mesh axis runs over, the one named last changes fastest.
Arguments:
- section_input: bfloat16 [2, 8192, 1536], P('segment', 'blk', 'mp'), may hold values from -36 to 36
- row_code: int32 [2, 8192], P('segment', 'blk'), may hold values from 0 to 255
- code_table: bfloat16 [2, 256, 1536], P('segment', None, 'mp'), may hold values from -6 to 6
- self_gain: float32 [2, 1536], P('segment'), may hold values from 0.1 to 1.9
- self_weights: bfloat16 [2, 3, 1536, 1536], P('segment', None, None, 'mp'), may hold values from -0.22963966 to 0.22963966
- self_out: bfloat16 [2, 1536, 1536], P('segment', 'mp'), may hold values from -0.15625 to 0.15625
- cross_gain: float32 [1536], replicated, may hold values from 0.1 to 1.9
- memory_gain: float32 [1536], replicated, may hold values from 0.1 to 1.9
- cross_weights: bfloat16 [3, 1536, 1536], P(None, None, 'mp'), may hold values from -0.22963966 to 0.22963966
- cross_out: bfloat16 [1536, 1536], P('mp'), may hold values from -0.15625 to 0.15625
Outputs:
- sections: bfloat16 [2, 8192, 1536], P('segment', 'blk', 'mp')
All inputs are finite; a program needn't handle non-finite values.
Results may differ from a plain program's by a relative error of at most 0.0085.
Values may be sent and summed in bfloat16 or wider, within the bound.
No kernel may reach another device: no remote copies, remote signals or barrier semaphores. Data moves between devices by JAX's collectives and lax.ppermute only.
A program may use at most 128 MiB of HBM per device.

v0:
```python
import math
import jax
import jax.numpy as jnp
from jax import lax
from jax.sharding import PartitionSpec as P

HEAD_DIM = 128


def shifted(value, axis, steps):
    count = lax.axis_size(axis)
    initial, last = (max(0, -steps), min(count, count - steps))
    return lax.ppermute(value, axis, [(source, source + steps) for source in range(initial, last)])


def rms_norm(values, gain):
    widened = values.astype(jnp.float32)
    meansq = jnp.mean(widened * widened, axis=-1, keepdims=True)
    return (widened * lax.rsqrt(meansq + 1e-05) * gain).astype(jnp.bfloat16)


def project(normed, weight):
    return jnp.dot(normed, weight, preferred_element_type=jnp.float32).astype(jnp.bfloat16)


def make_fold(queries):
    row_count = queries.shape[0]
    head_count = queries.shape[1] // HEAD_DIM
    grouped = queries.reshape(row_count, head_count, HEAD_DIM)
    factor = 1.0 / math.sqrt(HEAD_DIM)

    def fold(running, piece, start):
        piece_rows = piece.shape[1]
        block_rows = math.gcd(piece_rows, 1024)
        key_blocks = piece[0].reshape(piece_rows // block_rows, block_rows, head_count, HEAD_DIM)
        value_blocks = piece[1].reshape(piece_rows // block_rows, block_rows, head_count, HEAD_DIM)

        def absorb(current, blocks):
            running_max, running_sum, running_out = current
            key_block, value_block = blocks
            scores = (
                jnp.einsum("qhd,khd->qhk", grouped, key_block, preferred_element_type=jnp.float32)
                * factor
            )
            new_max = jnp.maximum(running_max, jnp.max(scores, axis=2))
            shrink = jnp.exp(running_max - new_max)
            weights = jnp.exp(scores - new_max[:, :, None])
            new_sum = running_sum * shrink + jnp.sum(weights, axis=2)
            new_out = running_out * shrink[:, :, None] + jnp.einsum(
                "qhk,khd->qhd",
                weights.astype(jnp.bfloat16),
                value_block,
                preferred_element_type=jnp.float32,
            )
            return ((new_max, new_sum, new_out), None)

        result, unused = lax.scan(absorb, running, (key_blocks, value_blocks))
        return result

    start_state = (
        jnp.full((row_count, head_count), -1e30, jnp.float32),
        jnp.zeros((row_count, head_count), jnp.float32),
        jnp.zeros((row_count, head_count, HEAD_DIM), jnp.float32),
    )
    return (fold, start_state)


def finish(running):
    running_max, running_sum, running_out = running
    merged = running_out / running_sum[:, :, None]
    return merged.reshape(merged.shape[0], merged.shape[1] * merged.shape[2]).astype(jnp.bfloat16)


def memory_projection(memory_full, memory_gain, cross_weights):
    memory_normed = rms_norm(memory_full, memory_gain)
    return jnp.stack(
        [project(memory_normed, cross_weights[1]), project(memory_normed, cross_weights[2])]
    )


def on_device(
    section_input,
    row_code,
    code_table,
    self_gain,
    self_weights,
    self_out,
    cross_gain,
    memory_gain,
    cross_weights,
    cross_out,
):
    local_rows = section_input.shape[1]
    codes_total = code_table.shape[1]
    matches = (
        row_code[0][:, None] == lax.broadcasted_iota(jnp.int32, (local_rows, codes_total), 1)
    ).astype(jnp.bfloat16)
    looked = jnp.dot(matches, code_table[0], preferred_element_type=jnp.float32)
    embedded = (section_input[0].astype(jnp.float32) + looked).astype(jnp.bfloat16)
    embedded_full = lax.all_gather(embedded, "mp", axis=1, tiled=True)
    normed = rms_norm(embedded_full, self_gain[0])
    self_queries = project(normed, self_weights[0, 0])
    self_pairs = jnp.stack(
        [project(normed, self_weights[0, 1]), project(normed, self_weights[0, 2])]
    )
    fold_self, self_start = make_fold(self_queries)
    self_running = fold_self(
        self_start, lax.all_gather(self_pairs, "blk", axis=1, tiled=True), jnp.int32(0)
    )
    partial_out = jnp.dot(finish(self_running), self_out[0], preferred_element_type=jnp.float32)
    reduced = lax.psum_scatter(
        partial_out.astype(jnp.bfloat16), "mp", scatter_dimension=1, tiled=True
    ).astype(jnp.float32)
    hidden_part = (embedded.astype(jnp.float32) + reduced).astype(jnp.bfloat16)
    hidden_full = lax.all_gather(hidden_part, "mp", axis=1, tiled=True)
    cross_queries = project(rms_norm(hidden_full, cross_gain), cross_weights[0])
    fold_cross, cross_start = make_fold(cross_queries)
    arrived = shifted(hidden_part, "segment", 1)
    memory_full = lax.all_gather(arrived, "mp", axis=1, tiled=True)
    memory_pairs = memory_projection(memory_full, memory_gain, cross_weights)
    crossed = fold_cross(
        cross_start, lax.all_gather(memory_pairs, "blk", axis=1, tiled=True), jnp.int32(0)
    )
    cross_partial = jnp.dot(finish(crossed), cross_out, preferred_element_type=jnp.float32)
    cross_reduced = lax.psum_scatter(
        cross_partial.astype(jnp.bfloat16), "mp", scatter_dimension=1, tiled=True
    ).astype(jnp.float32)
    decoded = (hidden_part.astype(jnp.float32) + cross_reduced).astype(jnp.bfloat16)
    chosen = jnp.where(lax.axis_index("segment") == 0, hidden_part, decoded)
    return chosen[None]


def solution(mesh):
    return jax.shard_map(
        on_device,
        mesh=mesh,
        in_specs=(
            P("segment", "blk", "mp"),
            P("segment", "blk"),
            P("segment", None, "mp"),
            P("segment", None),
            P("segment", None, None, "mp"),
            P("segment", "mp", None),
            P(),
            P(),
            P(None, None, "mp"),
            P("mp", None),
        ),
        out_specs=P("segment", "blk", "mp"),
        check_vma=False,
    )
```

profile of v0, /device:TPU:1, one launch (start us, length us, event | category | flops | bytes accessed | tf_op | source)
XLA Modules:
  0.0 598.6 jit_solution(17165010562332060110)
XLA Ops:
  8.0 10.3 %all_gather.15 = bf16[256,1536]{1,0:T(8,128)(2,1)S(1)} all-gather(bf16[256,384]{1,0:T(8,128)(2,1)S(1)} %fusion.90), channel_id=1, replica_groups=mesh['segment'=2,'blk'=32,'mp'=4] {'mp'}, dimensions={1}, use_global_device_ids=true | all-gather | bytes 983040 | tf_op jit(solution)/shard_map/all_gather | solution.py:100
  26.1 117.8 %all-gather.3.cloned.1.call-done = bf16[2,8192,384]{2,1,0:T(8,128)(2,1)} async-done(((bf16[2,256,384]{2,1,0:T(8,128)(2,1)}), bf16[2,8192,384]{2,1,0:T(8,128)(2,1)}) %all-gather.3.cloned.1.call-update) | async-done | bytes 12582928 | tf_op jit(solution)/shard_map/all_gather | solution.py:108
  143.9 10.2 %fusion.116 = (bf16[1,8192,384]{2,1,0:T(8,128)(2,1)}, bf16[1,8192,384]{2,1,0:T(8,128)(2,1)}) fusion(bf16[2,8192,384]{2,1,0:T(8,128)(2,1)} %all-gather.3.cloned.1.call-done), kind=kLoop, calls=%fused_computation.111 | loop fusion | bytes 25165824 | tf_op jit(solution)/shard_map/slice | solution.py:36
  154.1 16.6 %reshape.48 = bf16[8,1024,3,128]{3,2,1,0:T(4,128)(2,1)} reshape(bf16[1,8192,384]{2,1,0:T(8,128)(2,1)} %get-tuple-element.214) | data formatting | bytes 12582912 | tf_op jit(solution)/shard_map/reshape;squeeze | solution.py:35
  170.8 7.7 %copy.38 = bf16[8,1024,3,128]{3,1,2,0:T(8,128)(2,1)} copy(bf16[8,1024,3,128]{3,2,1,0:T(4,128)(2,1)} %reshape.48) | data formatting | bytes 12582912
  178.4 16.6 %reshape.49 = bf16[8,1024,3,128]{3,2,1,0:T(4,128)(2,1)} reshape(bf16[1,8192,384]{2,1,0:T(8,128)(2,1)} %get-tuple-element.213) | data formatting | bytes 12582912 | tf_op jit(solution)/shard_map/reshape;squeeze | solution.py:36
  195.1 13.0 %copy.40 = bf16[8,1024,3,128]{1,3,2,0:T(8,128)(2,1)} copy(bf16[8,1024,3,128]{3,2,1,0:T(4,128)(2,1)} %reshape.49) | data formatting | bytes 12582912
  208.1 65.1 %while.30 = (s32[]{:T(128)}, f32[256,3]{0,1:T(4,128)S(1)}, f32[256,3]{0,1:T(4,128)S(1)}, f32[256,3,128]{0,2,1:T(8,128)S(1)}, bf16[8,1024,3,128]{3,1,2,0:T(8,128)...) while((s32[]{:T(128)}, f32[256,3]{0,1:T(4,128)S(1)}, ...), condition=%wide.region_4.5_spmd.clone, body=%wide.region_1.4_spmd.clone.sunk | while | flops 409243392 | bytes 24626308 | solution.py:57
  208.1 3.4 bitcast_reduce_fusion.4
  211.5 2.6 fusion.137
  216.2 3.4 bitcast_reduce_fusion.4
  219.6 2.6 fusion.137
  224.4 3.4 bitcast_reduce_fusion.4
  227.8 2.6 fusion.137
  232.5 3.4 bitcast_reduce_fusion.4
  235.9 2.6 fusion.137
  240.6 3.4 bitcast_reduce_fusion.4
  244.0 2.6 fusion.137
  248.8 3.4 bitcast_reduce_fusion.4
  252.2 2.6 fusion.137
  256.9 3.4 bitcast_reduce_fusion.4
  260.3 2.6 fusion.137
  265.0 3.4 bitcast_reduce_fusion.4
  268.4 2.6 fusion.137
  275.1 20.2 %reduce-scatter.7.cloned.1.call-done = bf16[384,256]{1,0:T(8,128)(2,1)} async-done(((bf16[1536,256]{1,0:T(8,128)(2,1)}), bf16[384,256]{1,0:T(8,128)(2,1)}) %reduce-scatter.7.cloned.1.call-update) | async-done | bytes 196624
  296.4 4.5 collective-permute-start
  300.9 4.1 collective-permute-done
  305.0 8.7 %all_gather.17 = bf16[256,1536]{1,0:T(8,128)(2,1)S(1)} all-gather(bf16[256,384]{1,0:T(8,128)(2,1)S(1)} %collective-permute-done), channel_id=1, replica_groups=mesh['segment'=2,'blk'=32,'mp'=4] {'mp'}, dimensions={1}, use_global_device_ids=true | all-gather | bytes 983040 | tf_op jit(solution)/shard_map/all_gather | solution.py:119
  318.7 8.9 %all_gather.19 = bf16[256,1536]{1,0:T(8,128)(2,1)S(1)} all-gather(bf16[256,384]{1,0:T(8,128)(2,1)S(1)} %add_convert_fusion.1), channel_id=1, replica_groups=mesh['segment'=2,'blk'=32,'mp'=4] {'mp'}, dimensions={1}, use_global_device_ids=true | all-gather | bytes 983040 | tf_op jit(solution)/shard_map/all_gather | solution.py:115
  330.0 108.6 %all-gather.5.cloned.1.call-done = bf16[2,8192,384]{2,1,0:T(8,128)(2,1)} async-done(((bf16[2,256,384]{2,1,0:T(8,128)(2,1)}), bf16[2,8192,384]{2,1,0:T(8,128)(2,1)}) %all-gather.5.cloned.1.call-update) | async-done | bytes 12582928 | tf_op jit(solution)/shard_map/all_gather | solution.py:122
  438.6 10.2 %fusion.115 = (bf16[1,8192,384]{2,1,0:T(8,128)(2,1)}, bf16[1,8192,384]{2,1,0:T(8,128)(2,1)}) fusion(bf16[2,8192,384]{2,1,0:T(8,128)(2,1)} %all-gather.5.cloned.1.call-done), kind=kLoop, calls=%fused_computation.110 | loop fusion | bytes 25165824 | tf_op jit(solution)/shard_map/slice | solution.py:36
  448.8 16.6 %reshape.50 = bf16[8,1024,3,128]{3,2,1,0:T(4,128)(2,1)} reshape(bf16[1,8192,384]{2,1,0:T(8,128)(2,1)} %get-tuple-element.212) | data formatting | bytes 12582912 | tf_op jit(solution)/shard_map/reshape;squeeze | solution.py:35
  465.5 7.7 %copy.44 = bf16[8,1024,3,128]{3,1,2,0:T(8,128)(2,1)} copy(bf16[8,1024,3,128]{3,2,1,0:T(4,128)(2,1)} %reshape.50) | data formatting | bytes 12582912
  473.1 16.6 %reshape.51 = bf16[8,1024,3,128]{3,2,1,0:T(4,128)(2,1)} reshape(bf16[1,8192,384]{2,1,0:T(8,128)(2,1)} %get-tuple-element.211) | data formatting | bytes 12582912 | tf_op jit(solution)/shard_map/reshape;squeeze | solution.py:36
  489.8 13.0 %copy.46 = bf16[8,1024,3,128]{1,3,2,0:T(8,128)(2,1)} copy(bf16[8,1024,3,128]{3,2,1,0:T(4,128)(2,1)} %reshape.51) | data formatting | bytes 12582912
  502.8 65.2 %while.31 = (s32[]{:T(128)}, f32[256,3]{0,1:T(4,128)S(1)}, f32[256,3]{0,1:T(4,128)S(1)}, f32[256,3,128]{0,2,1:T(8,128)S(1)}, bf16[8,1024,3,128]{3,1,2,0:T(8,128)...) while((s32[]{:T(128)}, f32[256,3]{0,1:T(4,128)S(1)}, ...), condition=%wide.region_11.12_spmd.clone, body=%wide.region_8.11_spmd.clone.sunk | while | flops 409243392 | bytes 24626308 | solution.py:57
  502.8 3.5 bitcast_reduce_fusion.5
  506.3 2.6 fusion.143
  511.1 3.4 bitcast_reduce_fusion.5
  514.4 2.6 fusion.143
  519.2 3.4 bitcast_reduce_fusion.5
  522.6 2.6 fusion.143
  527.3 3.4 bitcast_reduce_fusion.5
  535.5 3.4 bitcast_reduce_fusion.5
  543.6 3.4 bitcast_reduce_fusion.5
  551.7 3.4 bitcast_reduce_fusion.5
  559.9 3.4 bitcast_reduce_fusion.5
  569.8 20.4 %reduce-scatter.9.cloned.1.call-done = bf16[384,256]{1,0:T(8,128)(2,1)} async-done(((bf16[1536,256]{1,0:T(8,128)(2,1)}), bf16[384,256]{1,0:T(8,128)(2,1)}) %reduce-scatter.9.cloned.1.call-update) | async-done | bytes 196624
  (155 shorter events, 70.4 us)
Async XLA Ops:
  6.5 266.7 %copy-start = (bf16[1,384,1536]{2,1,0:T(8,128)(2,1)S(1)}, bf16[1,384,1536]{2,1,0:T(8,128)(2,1)}, u32[]{:S(2)}) copy-start(bf16[1,384,1536]{2,1,0:T(8,128)(2,1)} %param.19) | copy-start | bytes 3538948
  6.5 137.4 %all-gather.3.cloned.1.call-start = ((), (), s32[]{:S(2)}) async-start(), calls=%async_computation.2 | async-start | bytes 12976128 | tf_op jit(solution)/shard_map/all_gather | solution.py:108
  23.8 271.5 %reduce-scatter.7.cloned.1.call-start = ((), (), s32[]{:S(2)}) async-start(), calls=%async_computation.4 | async-start | bytes 983040
  211.5 2.8 copy-start.2
  219.6 2.8 copy-start.2
  227.8 2.8 copy-start.2
  235.9 2.8 copy-start.2
  244.0 2.8 copy-start.2
  252.2 2.8 copy-start.2
  260.3 2.8 copy-start.2
  268.4 2.8 copy-start.2
  273.2 40.8 %copy-start.5 = (f32[1536]{0:T(1024)S(1)}, f32[1536]{0:T(1024)}, u32[]{:S(2)}) copy-start(f32[1536]{0:T(1024)} %param.21) | copy-start | bytes 18436
  275.0 163.6 %all-gather.5.cloned.1.call-start = ((), (), s32[]{:S(2)}) async-start(), calls=%async_computation.3 | async-start | bytes 12976128 | tf_op jit(solution)/shard_map/all_gather | solution.py:122
  296.4 8.6 %collective-permute-start = (bf16[256,384]{1,0:T(8,128)(2,1)S(1)}, bf16[256,384]{1,0:T(8,128)(2,1)S(1)}, u32[]{:S(2)}, u32[]{:S(2)}) collective-permute-start(bf16[256,384]{1,0:T(8,128)(2,1)S(1)} %add_convert_fusion.1), channel_id=1, source_target_pairs={{0,128},{1,129},{2,130},{3,131},{4,132},{5,133},{6,134},{7,135},{8... | collective-permute-start | bytes 589832 | tf_op jit(solution)/shard_map/ppermute | solution.py:13
  315.9 11.9 %copy-start.6 = (f32[1536]{0:T(1024)S(1)}, f32[1536]{0:T(1024)}, u32[]{:S(2)}) copy-start(f32[1536]{0:T(1024)} %param.20) | copy-start | bytes 18436
  318.6 271.6 %reduce-scatter.9.cloned.1.call-start = ((), (), s32[]{:S(2)}) async-start(), calls=%async_computation.5 | async-start | bytes 983040
  502.8 65.2 %copy-start.4 = (bf16[384,1536]{1,0:T(8,128)(2,1)S(1)}, bf16[384,1536]{1,0:T(8,128)(2,1)}, u32[]{:S(2)}) copy-start(bf16[384,1536]{1,0:T(8,128)(2,1)} %param.23) | copy-start | bytes 3538948
  506.3 2.8 copy-start.3
  514.4 2.8 copy-start.3
  522.6 2.8 copy-start.3
  530.7 2.8 copy-start.3
  538.8 2.8 copy-start.3
  547.0 2.8 copy-start.3
  555.1 2.8 copy-start.3
  563.2 2.8 copy-start.3
  568.0 24.1 %copy-start.1 = (bf16[1,384,1536]{2,1,0:T(8,128)(2,1)S(1)}, bf16[1,384,1536]{2,1,0:T(8,128)(2,1)}, u32[]{:S(2)}) copy-start(bf16[1,384,1536]{2,1,0:T(8,128)(2,1)} %param.19) | copy-start | bytes 3538948
Sparse Core Ops, SparseCore 0:
  23.9 119.9 all-gather.2
  275.1 20.1 reduce-scatter.6
  318.7 119.8 all-gather.4
  569.9 20.2 reduce-scatter.8
where the time goes:
time: 603 us; the launch traced here: 599 us
  waiting for transfers between devices  271 us (45%)
  local copies, waits for them, and re-layouts  137 us (23%)
  matrix products  98.3 us (16%)
  other arithmetic  45.4 us (8%)
  blocking collectives  27.8 us (5%)
  between operations  13.4 us (2%)
    all_gather x1, waiting for transfers between devices, on_device(): lax.all_gather(self_pairs, 'blk', axis=1, tiled=True)  118 us
    all_gather x1, waiting for transfers between devices, on_device(): lax.all_gather(memory_pairs, 'blk', axis=1, tiled=True)  109 us
    dot_general x16, matrix products, absorb(): jnp.einsum('qhd,khd->qhk', grouped, key_block, preferred_element_type=jnp...  54.2 us
    unnamed x20, local copies, waits for them, and re-layouts  46.3 us
    reduce_sum x16, other arithmetic, absorb(): new_sum = running_sum * shrink + jnp.sum(weights, axis=2)  41.1 us
    unnamed x6, waiting for transfers between devices  40.7 us
    another operation x2, local copies, waits for them, and re-layouts, fold(): piece[0].reshape(piece_rows // block_rows, block_rows, head_count, HEAD_DIM)  33.3 us
    another operation x2, local copies, waits for them, and re-layouts, fold(): piece[1].reshape(piece_rows // block_rows, block_rows, head_count, HEAD_DIM)  33.3 us
  transfers between devices with their start and end apart: 5, of which 5 were waited for; matrix products, arithmetic and copies ran while one was open for 1% of the time, Pallas kernels for 0%

commit v1 on v0

--- a/solution.py
+++ b/solution.py
@@ -105,7 +105,11 @@
     )
     fold_self, self_start = make_fold(self_queries)
     self_running = fold_self(
-        self_start, lax.all_gather(self_pairs, "blk", axis=1, tiled=True), jnp.int32(0)
+        self_start,
+        jnp.concatenate(
+            lax.all_to_all(jnp.stack([self_pairs] * lax.axis_size("blk")), "blk", 0, 0), axis=1
+        ),
+        jnp.int32(0),
     )
     partial_out = jnp.dot(finish(self_running), self_out[0], preferred_element_type=jnp.float32)
     reduced = lax.psum_scatter(

time: 603 us -> 803 us (1.33)
  waiting for transfers between devices: 271 us -> 457 us
  starting transfers between devices: 4.58 us -> 15.5 us
    all_to_all x0 -> x1, waiting for transfers between devices: none -> 287 us  [on_device(): lax.all_to_all(jnp.stack([self_pairs] * lax.axis_size('blk')), 'blk', 0, 0)]
    all_gather x1 -> x0, waiting for transfers between devices: 118 us -> none  [on_device(): lax.all_gather(self_pairs, 'blk', axis=1, tiled=True)]
    unnamed x6 -> x5, waiting for transfers between devices: 40.7 us -> 56.9 us
    all_to_all x0 -> x1, starting transfers between devices: none -> 10.9 us  [on_device(): lax.all_to_all(jnp.stack([self_pairs] * lax.axis_size('blk')), 'blk', 0, 0)]
    slice x2 -> x3, local copies, waits for them, and re-layouts: 20.4 us -> 27.4 us  [fold(): piece[1].reshape(piece_rows // block_rows, block_rows, head_count, HEAD_DIM)]
where the time goes in v1:
time: 803 us; the launch traced here: 799 us
  waiting for transfers between devices  457 us (57%)
  local copies, waits for them, and re-layouts  143 us (18%)
  matrix products  98.3 us (12%)
  other arithmetic  44.6 us (6%)
  blocking collectives  27.7 us (3%)
  starting transfers between devices  15.5 us (2%)
  between operations  13.4 us (2%)
    all_to_all x1, waiting for transfers between devices, on_device(): lax.all_to_all(jnp.stack([self_pairs] * lax.axis_size('blk')), 'blk', 0, 0)  287 us
    all_gather x1, waiting for transfers between devices, on_device(): lax.all_gather(memory_pairs, 'blk', axis=1, tiled=True)  109 us
    unnamed x5, waiting for transfers between devices  56.9 us
    dot_general x16, matrix products, absorb(): jnp.einsum('qhd,khd->qhk', grouped, key_block, preferred_element_type=jnp...  54.2 us
    unnamed x20, local copies, waits for them, and re-layouts  43.6 us
    reduce_sum x16, other arithmetic, absorb(): new_sum = running_sum * shrink + jnp.sum(weights, axis=2)  41.1 us
    dot_general x16, matrix products, absorb(): jnp.einsum('qhk,khd->qhd', weights.astype(jnp.bfloat16), value_block, pre...  30.2 us
    slice x3, local copies, waits for them, and re-layouts, fold(): piece[1].reshape(piece_rows // block_rows, block_rows, head_count, HEAD_DIM)  27.4 us
  transfers between devices with their start and end apart: 5, of which 5 were waited for; matrix products, arithmetic and copies ran while one was open for 1% of the time, Pallas kernels for 0%

profile of v1, /device:TPU:1, one launch (start us, length us, event | category | flops | bytes accessed | tf_op | source)
XLA Modules:
  0.0 799.2 jit_solution(14679531631344974068)
XLA Ops:
  8.0 10.3 %all_gather.12 = bf16[256,1536]{1,0:T(8,128)(2,1)S(1)} all-gather(bf16[256,384]{1,0:T(8,128)(2,1)S(1)} %fusion.90), channel_id=1, replica_groups=mesh['segment'=2,'blk'=32,'mp'=4] {'mp'}, dimensions={1}, use_global_device_ids=true | all-gather | bytes 983040 | tf_op jit(solution)/shard_map/all_gather | solution.py:100
  23.2 6.1 stack.17
  29.3 10.9 %all-to-all-start = ((bf16[32,2,256,384]{2,3,1,0:T(8,128)(2,1)}), bf16[32,2,256,384]{2,3,1,0:T(8,128)(2,1)}, u32[]{:S(2)}, u32[]{:S(2)}) async-start(bf16[32,2,256,384]{2,3,1,0:T(8,128)(2,1)} %stack.17), calls=%async_computation | async-start | bytes 25165824 | tf_op jit(solution)/shard_map/all_to_all | solution.py:110
  42.7 286.9 %all-to-all-done = bf16[32,2,256,384]{2,3,1,0:T(8,128)(2,1)} async-done(((bf16[32,2,256,384]{2,3,1,0:T(8,128)(2,1)}), bf16[32,2,256,384]{2,3,1,0:T(8,128)(2,1)}, u32[]{:S(2)}, u32[]{:S(2)}) %all-to-all-start) | async-done | bytes 12582944 | tf_op jit(solution)/shard_map/all_to_all | solution.py:110
  329.6 8.3 %fusion.116 = (bf16[1,32,256,384]{2,3,0,1:T(8,128)(2,1)}, bf16[1,32,256,384]{2,3,0,1:T(8,128)(2,1)S(1)}) fusion(bf16[2,32,256,384]{2,3,0,1:T(8,128)(2,1)} %bitcast.7), kind=kLoop, calls=%fused_computation.111 | loop fusion | bytes 25165824 | tf_op jit(solution)/shard_map/slice | solution.py:36
  337.8 6.3 copy.33
  344.2 10.8 %reshape_squeeze.12 = bf16[8,1024,3,128]{1,0,3,2:T(8,128)(2,1)} reshape(bf16[1,32,256,384]{2,1,3,0:T(8,128)(2,1)} %copy.33) | data formatting | bytes 12582912 | tf_op jit(solution)/shard_map/reshape;squeeze | solution.py:35
  354.9 9.1 %copy.36 = bf16[8,1024,3,128]{3,1,2,0:T(8,128)(2,1)} copy(bf16[8,1024,3,128]{1,0,3,2:T(8,128)(2,1)} %reshape_squeeze.12) | data formatting | bytes 12582912
  364.1 9.0 %copy.35 = bf16[1,32,256,384]{2,1,3,0:T(8,128)(2,1)} copy(bf16[1,32,256,384]{2,3,0,1:T(8,128)(2,1)} %get-tuple-element.213) | data formatting | bytes 12582912 | tf_op jit(solution)/shard_map/slice | solution.py:36
  373.0 10.7 %reshape_squeeze.13 = bf16[8,1024,3,128]{1,0,3,2:T(8,128)(2,1)} reshape(bf16[1,32,256,384]{2,1,3,0:T(8,128)(2,1)} %copy.35) | data formatting | bytes 12582912 | tf_op jit(solution)/shard_map/reshape;squeeze | solution.py:36
  383.7 8.9 %copy.38 = bf16[8,1024,3,128]{1,3,2,0:T(8,128)(2,1)} copy(bf16[8,1024,3,128]{1,0,3,2:T(8,128)(2,1)} %reshape_squeeze.13) | data formatting | bytes 12582912
  392.7 65.1 %while.30 = (s32[]{:T(128)}, f32[256,3]{0,1:T(4,128)S(1)}, f32[256,3]{0,1:T(4,128)S(1)}, f32[256,3,128]{0,2,1:T(8,128)S(1)}, bf16[8,1024,3,128]{3,1,2,0:T(8,128)...) while((s32[]{:T(128)}, f32[256,3]{0,1:T(4,128)S(1)}, ...), condition=%wide.region_4.5_spmd.clone, body=%wide.region_1.4_spmd.clone.sunk | while | flops 409243392 | bytes 24626308 | solution.py:57
  392.7 3.4 bitcast_reduce_fusion.4
  396.1 2.6 fusion.137
  400.8 3.4 bitcast_reduce_fusion.4
  404.2 2.6 fusion.137
  408.9 3.4 bitcast_reduce_fusion.4
  412.3 2.6 fusion.137
  417.1 3.4 bitcast_reduce_fusion.4
  420.5 2.6 fusion.137
  425.2 3.4 bitcast_reduce_fusion.4
  428.6 2.6 fusion.137
  433.4 3.4 bitcast_reduce_fusion.4
  441.5 3.4 bitcast_reduce_fusion.4
  444.9 2.6 fusion.137
  449.6 3.4 bitcast_reduce_fusion.4
  453.0 2.6 fusion.137
  459.6 36.4 %reduce-scatter.7.cloned.1.call-done = bf16[384,256]{1,0:T(8,128)(2,1)} async-done(((bf16[1536,256]{1,0:T(8,128)(2,1)}), bf16[384,256]{1,0:T(8,128)(2,1)}) %reduce-scatter.7.cloned.1.call-update) | async-done | bytes 196624
  497.2 4.3 collective-permute-start
  501.5 4.1 collective-permute-done
  505.6 8.7 %all_gather.13 = bf16[256,1536]{1,0:T(8,128)(2,1)S(1)} all-gather(bf16[256,384]{1,0:T(8,128)(2,1)S(1)} %collective-permute-done), channel_id=1, replica_groups=mesh['segment'=2,'blk'=32,'mp'=4] {'mp'}, dimensions={1}, use_global_device_ids=true | all-gather | bytes 983040 | tf_op jit(solution)/shard_map/all_gather | solution.py:123
  519.2 8.7 %all_gather.15 = bf16[256,1536]{1,0:T(8,128)(2,1)S(1)} all-gather(bf16[256,384]{1,0:T(8,128)(2,1)S(1)} %add_convert_fusion.1), channel_id=1, replica_groups=mesh['segment'=2,'blk'=32,'mp'=4] {'mp'}, dimensions={1}, use_global_device_ids=true | all-gather | bytes 983040 | tf_op jit(solution)/shard_map/all_gather | solution.py:119
  530.4 108.8 %all-gather.2.cloned.1.call-done = bf16[2,8192,384]{2,1,0:T(8,128)(2,1)} async-done(((bf16[2,256,384]{2,1,0:T(8,128)(2,1)}), bf16[2,8192,384]{2,1,0:T(8,128)(2,1)}) %all-gather.2.cloned.1.call-update) | async-done | bytes 12582928 | tf_op jit(solution)/shard_map/all_gather | solution.py:126
  639.2 10.2 %fusion.115 = (bf16[1,8192,384]{2,1,0:T(8,128)(2,1)}, bf16[1,8192,384]{2,1,0:T(8,128)(2,1)}) fusion(bf16[2,8192,384]{2,1,0:T(8,128)(2,1)} %all-gather.2.cloned.1.call-done), kind=kLoop, calls=%fused_computation.110 | loop fusion | bytes 25165824 | tf_op jit(solution)/shard_map/slice | solution.py:36
  649.4 16.6 %reshape.59 = bf16[8,1024,3,128]{3,2,1,0:T(4,128)(2,1)} reshape(bf16[1,8192,384]{2,1,0:T(8,128)(2,1)} %get-tuple-element.212) | data formatting | bytes 12582912 | tf_op jit(solution)/shard_map/reshape;squeeze | solution.py:35
  666.0 7.7 copy.42
  673.7 16.6 %reshape.60 = bf16[8,1024,3,128]{3,2,1,0:T(4,128)(2,1)} reshape(bf16[1,8192,384]{2,1,0:T(8,128)(2,1)} %get-tuple-element.211) | data formatting | bytes 12582912 | tf_op jit(solution)/shard_map/reshape;squeeze | solution.py:36
  690.3 13.0 %copy.44 = bf16[8,1024,3,128]{1,3,2,0:T(8,128)(2,1)} copy(bf16[8,1024,3,128]{3,2,1,0:T(4,128)(2,1)} %reshape.60) | data formatting | bytes 12582912
  703.4 65.2 %while.31 = (s32[]{:T(128)}, f32[256,3]{0,1:T(4,128)S(1)}, f32[256,3]{0,1:T(4,128)S(1)}, f32[256,3,128]{0,2,1:T(8,128)S(1)}, bf16[8,1024,3,128]{3,1,2,0:T(8,128)...) while((s32[]{:T(128)}, f32[256,3]{0,1:T(4,128)S(1)}, ...), condition=%wide.region_11.12_spmd.clone, body=%wide.region_8.11_spmd.clone.sunk | while | flops 409243392 | bytes 24626308 | solution.py:57
  703.4 3.5 bitcast_reduce_fusion.5
  711.6 3.4 bitcast_reduce_fusion.5
  719.8 3.4 bitcast_reduce_fusion.5
  727.9 3.4 bitcast_reduce_fusion.5
  736.0 3.4 bitcast_reduce_fusion.5
  744.2 3.4 bitcast_reduce_fusion.5
  752.3 3.4 bitcast_reduce_fusion.5
  760.4 3.4 bitcast_reduce_fusion.5
  770.4 20.4 %reduce-scatter.9.cloned.1.call-done = bf16[384,256]{1,0:T(8,128)(2,1)} async-done(((bf16[1536,256]{1,0:T(8,128)(2,1)}), bf16[384,256]{1,0:T(8,128)(2,1)}) %reduce-scatter.9.cloned.1.call-update) | async-done | bytes 196624
  (158 shorter events, 80.2 us)
Async XLA Ops:
  6.5 451.3 %copy-start = (bf16[1,384,1536]{2,1,0:T(8,128)(2,1)S(1)}, bf16[1,384,1536]{2,1,0:T(8,128)(2,1)}, u32[]{:S(2)}) copy-start(bf16[1,384,1536]{2,1,0:T(8,128)(2,1)} %param.19) | copy-start | bytes 3538948
  29.3 300.3 %all-to-all-start = ((bf16[32,2,256,384]{2,3,1,0:T(8,128)(2,1)}), bf16[32,2,256,384]{2,3,1,0:T(8,128)(2,1)}, u32[]{:S(2)}, u32[]{:S(2)}) async-start(bf16[32,2,256,384]{2,3,1,0:T(8,128)(2,1)} %stack.17), calls=%async_computation | async-start | bytes 25165824 | tf_op jit(solution)/shard_map/all_to_all | solution.py:110
  40.2 455.9 %reduce-scatter.7.cloned.1.call-start = ((), (), s32[]{:S(2)}) async-start(), calls=%async_computation.4 | async-start | bytes 983040
  396.1 2.8 copy-start.2
  404.2 2.8 copy-start.2
  412.3 2.8 copy-start.2
  420.5 2.8 copy-start.2
  428.6 2.8 copy-start.2
  436.7 2.8 copy-start.2
  444.9 2.8 copy-start.2
  453.0 2.8 copy-start.2
  457.8 56.7 %copy-start.5 = (f32[1536]{0:T(1024)S(1)}, f32[1536]{0:T(1024)}, u32[]{:S(2)}) copy-start(f32[1536]{0:T(1024)} %param.21) | copy-start | bytes 18436
  459.6 179.6 %all-gather.2.cloned.1.call-start = ((), (), s32[]{:S(2)}) async-start(), calls=%async_computation.3 | async-start | bytes 12976128 | tf_op jit(solution)/shard_map/all_gather | solution.py:126
  497.2 8.3 %collective-permute-start = (bf16[256,384]{1,0:T(8,128)(2,1)S(1)}, bf16[256,384]{1,0:T(8,128)(2,1)S(1)}, u32[]{:S(2)}, u32[]{:S(2)}) collective-permute-start(bf16[256,384]{1,0:T(8,128)(2,1)S(1)} %add_convert_fusion.1), channel_id=1, source_target_pairs={{0,128},{1,129},{2,130},{3,131},{4,132},{5,133},{6,134},{7,135},{8... | collective-permute-start | bytes 589832 | tf_op jit(solution)/shard_map/ppermute | solution.py:13
  516.4 11.8 %copy-start.6 = (f32[1536]{0:T(1024)S(1)}, f32[1536]{0:T(1024)}, u32[]{:S(2)}) copy-start(f32[1536]{0:T(1024)} %param.20) | copy-start | bytes 18436
  519.1 271.7 %reduce-scatter.9.cloned.1.call-start = ((), (), s32[]{:S(2)}) async-start(), calls=%async_computation.5 | async-start | bytes 983040
  703.4 65.2 %copy-start.4 = (bf16[384,1536]{1,0:T(8,128)(2,1)S(1)}, bf16[384,1536]{1,0:T(8,128)(2,1)}, u32[]{:S(2)}) copy-start(bf16[384,1536]{1,0:T(8,128)(2,1)} %param.23) | copy-start | bytes 3538948
  706.9 2.8 copy-start.3
  715.0 2.8 copy-start.3
  723.1 2.8 copy-start.3
  731.3 2.8 copy-start.3
  739.4 2.8 copy-start.3
  747.5 2.8 copy-start.3
  755.7 2.8 copy-start.3
  763.8 2.8 copy-start.3
  768.6 24.1 %copy-start.1 = (bf16[1,384,1536]{2,1,0:T(8,128)(2,1)S(1)}, bf16[1,384,1536]{2,1,0:T(8,128)(2,1)}, u32[]{:S(2)}) copy-start(bf16[1,384,1536]{2,1,0:T(8,128)(2,1)} %param.19) | copy-start | bytes 3538948
Sparse Core Ops, SparseCore 0:
  459.7 36.3 reduce-scatter.6
  519.2 119.9 all-gather.1
  770.5 20.2 reduce-scatter.8
